TPU v7x, 256 devices: a whole 4x4x8 slice. The times are simulated.
256 devices in a mesh: target: 32 (over x_lo, z, core), surface: 8 (over x_hi, y).
Axes of the slice: x: 4 (x_hi: 2, x_lo: 2; x = x_hi * 2 + x_lo), y: 4, z: 8, core: 2. Of those that a mesh axis runs over, the one named last changes fastest.
Arguments:
- response: float32 [64, 32, 32, 512], P('target', None, 'surface'), may hold values from -6 to 6
- data_spectra: bfloat16 [32, 16, 2, 32, 32, 256], P('target', None, None, 'surface'), may hold values from -0.01171875 to 0.01171875
- observed: bfloat16 [32, 2, 32, 32, 256], P('target', None, None, 'surface'), may hold values from -6 to 6
- block_lists: int32 [32, 16], replicated, may hold values from 0 to 63, as said below
Outputs:
- response_next: float32 [64, 32, 32, 512], P('target', None, 'surface')
- response_copy: bfloat16 [64, 32, 32, 512], P('target', None, 'surface')
- residual: float32 [32, 2, 32, 32, 256], P('target', None, None, 'surface')
Inputs may be any that keep to these rules, and one draw needn't show every extreme that they name: `block_lists`: block b is owned by index b // 2 of target. Each tile lists 16 blocks, no two of the same owner.
All inputs are finite; a program needn't handle non-finite values.
Results may differ from a plain program's by a relative error of at most 0.0048.
Values may be sent and summed in bfloat16 or wider, within the bound.
No kernel may reach another device: no remote copies, remote signals or barrier semaphores. Data moves between devices by JAX's collectives and lax.ppermute only.
A program may use at most 128 MiB of HBM per device.

v0:
```python
import math
import jax
import jax.numpy as jnp
from jax import lax
from jax.sharding import PartitionSpec as P

step_length = 0.5


def make_table(samples):
    freqs = samples // 2
    sample_index = lax.broadcasted_iota(jnp.int32, (samples, freqs), 0)
    freq_index = lax.broadcasted_iota(jnp.int32, (samples, freqs), 1)
    phase = (sample_index * freq_index % samples).astype(jnp.float32) * (2.0 * math.pi / samples)
    return jnp.concatenate([jnp.cos(phase), -jnp.sin(phase)], axis=1)


def contract(spec, listed):
    return jnp.einsum("lakf,lkrf->arf", spec, listed, preferred_element_type=jnp.float32)


def correlate(misfit_part, listed):
    return jnp.einsum("arf,lkrf->lakf", misfit_part, listed, preferred_element_type=jnp.float32)


def per_device(response, data_spectra, observed, block_lists):
    owners = lax.axis_size("target")
    my_index = lax.axis_index("target")
    owned = response.shape[0]
    samples = response.shape[3]
    freqs = samples // 2
    dft_table = make_table(samples)
    table_half = dft_table.astype(jnp.bfloat16)
    own_ids = lax.dynamic_slice_in_dim(block_lists, my_index, 1, 0)[0]
    own_owner = own_ids // owned
    wanted = block_lists // owned == my_index
    present = jnp.any(wanted, axis=1)
    slot_for = jnp.sum(jnp.where(wanted, block_lists % owned, 0), axis=1)
    picker = (
        (slot_for[None, :] == jnp.arange(owned, dtype=jnp.int32)[:, None]) & present[None, :]
    ).astype(jnp.float32)
    present_rows = present[:, None, None, None]
    zero_half = jnp.zeros((), jnp.bfloat16)
    copy_now = response.astype(jnp.bfloat16)
    outgoing = jnp.where(present_rows, copy_now[slot_for], zero_half)
    arrived = lax.all_to_all(outgoing, "target", split_axis=0, concat_axis=0, tiled=True)
    spectra = jnp.dot(arrived[own_owner], table_half, preferred_element_type=jnp.float32).astype(
        jnp.bfloat16
    )
    listed_data = data_spectra[0]
    spec_real = spectra[..., :freqs]
    spec_imag = spectra[..., freqs:]
    data_real = listed_data[:, 0]
    data_imag = listed_data[:, 1]
    partial_value = jnp.stack(
        [
            contract(spec_real, data_real) - contract(spec_imag, data_imag),
            contract(spec_real, data_imag) + contract(spec_imag, data_real),
        ]
    )
    observed_share = observed[0].astype(jnp.float32)
    summed_share = lax.psum_scatter(partial_value, "surface", scatter_dimension=2, tiled=True)
    residual_share = observed_share - summed_share
    misfit = lax.all_gather(residual_share.astype(jnp.bfloat16), "surface", axis=2, tiled=True)
    misfit_real = misfit[0]
    misfit_imag = misfit[1]
    grad_spectra = jnp.concatenate(
        [
            -(correlate(misfit_real, data_real) + correlate(misfit_imag, data_imag)),
            correlate(misfit_real, data_imag) - correlate(misfit_imag, data_real),
        ],
        axis=-1,
    )
    grad_time = jnp.dot(grad_spectra, dft_table.T, precision=lax.Precision.HIGHEST)
    returning = jnp.zeros((owners,) + grad_time.shape[1:], jnp.float32).at[own_owner].set(grad_time)
    received = lax.all_to_all(returning, "target", split_axis=0, concat_axis=0, tiled=True)
    flat = received.reshape(owners, -1)
    gradient = jnp.dot(picker, flat, precision=lax.Precision.HIGHEST).reshape(response.shape)
    response_next = response - step_length * gradient
    return (response_next, response_next.astype(jnp.bfloat16), residual_share[None])


def solution(mesh):
    return jax.shard_map(
        per_device,
        mesh=mesh,
        in_specs=(
            P("target", None, "surface", None),
            P("target", None, None, "surface", None, None),
            P("target", None, None, "surface", None),
            P(),
        ),
        out_specs=(
            P("target", None, "surface", None),
            P("target", None, "surface", None),
            P("target", None, None, "surface", None),
        ),
        check_vma=False,
    )
```

profile of v0, /device:TPU:96, one launch (start us, length us, event | category | flops | bytes accessed | tf_op | source)
XLA Modules:
  0.0 651.4 jit_solution(16325674682704119219)
XLA Ops:
  9.8 5.6 gather_fusion
  15.4 5.9 broadcast_select_fusion
  21.3 8.9 %all-to-all-start = ((bf16[32,32,4,512]{3,2,1,0:T(4,128)(2,1)}), bf16[32,32,4,512]{3,2,1,0:T(4,128)(2,1)}, u32[]{:S(2)}, u32[]{:S(2)}) async-start(bf16[32,32,4,512]{3,2,1,0:T(4,128)(2,1)} %broadcast_select_fusion), calls=%async_computation | async-start | bytes 8388608 | tf_op jit(solution)/shard_map/all_to_all | solution.py:46
  30.5 12.0 %copy.72 = bf16[1,16,2,4,32,256]{4,1,3,5,2,0:T(8,128)(2,1)} copy(bf16[1,16,2,4,32,256]{5,4,3,2,1,0:T(8,128)(2,1)S(1)} %copy-done.4) | data formatting | bytes 4194304 | tf_op args[1]
  44.8 81.4 %all-to-all-done = bf16[32,32,4,512]{3,2,1,0:T(4,128)(2,1)} async-done(((bf16[32,32,4,512]{3,2,1,0:T(4,128)(2,1)}), bf16[32,32,4,512]{3,2,1,0:T(4,128)(2,1)}, u32[]{:S(2)}, u32[]{:S(2)}) %all-to-all-start) | async-done | bytes 4194336 | tf_op jit(solution)/shard_map/all_to_all | solution.py:46
  126.2 4.5 gather_fusion.1
  132.3 6.5 copy.73
  138.8 6.7 %copy.74 = bf16[16,32,4,256]{1,0,2,3:T(8,128)(2,1)} copy(bf16[16,32,4,256]{3,1,2,0:T(8,128)(2,1)S(1)} %get-tuple-element.21) | data formatting | bytes 2097152 | tf_op jit(solution)/shard_map/slice | solution.py:52
  145.6 6.9 %fusion.9 = f32[256,32,32,1]{2,1,3,0:T(8,128)} fusion(bf16[16,32,4,256]{1,0,2,3:T(8,128)(2,1)} %copy.74, bf16[16,2,4,32,256]{3,0,2,4,1:T(8,128)(2,1)} %bitcast.108), kind=kOutput, calls=%fused_computation.20 | convolution fusion | flops 33554432 | bytes 9437184 | tf_op jit(solution)/shard_map/lakf,lkrf->arf/dot_general | solution.py:19
  152.5 3.7 fusion.10
  156.2 5.7 fusion.6
  165.1 6.5 pad_maximum_fusion
  171.6 8.0 %copy.77 = f32[2,32,32,256]{3,1,0,2:T(8,128)} copy(f32[2,32,32,256]{2,1,3,0:T(8,128)} %pad_maximum_fusion) | data formatting | bytes 4194304 | tf_op jit(solution)/shard_map/stack | solution.py:55
  179.7 79.2 %reduce-scatter.2.cloned.1.call-done = f32[2,32,4,256]{3,1,0,2:T(8,128)} async-done(((f32[2,32,32,256]{3,1,0,2:T(8,128)}), f32[2,32,4,256]{3,1,0,2:T(8,128)}) %reduce-scatter.2.cloned.1.call-update) | async-done | bytes 262160 | tf_op jit(solution)/shard_map/reduce_scatter | solution.py:62
  260.5 51.9 %all-gather.2.cloned.1.call-done = bf16[2,32,32,256]{3,1,0,2:T(8,128)(2,1)} async-done(((bf16[2,32,4,256]{3,1,0,2:T(8,128)(2,1)}), bf16[2,32,32,256]{3,1,0,2:T(8,128)(2,1)}) %all-gather.2.cloned.1.call-update) | async-done | bytes 1048592 | tf_op jit(solution)/shard_map/all_gather | solution.py:64
  314.6 14.5 %copy.97 = bf16[1,32,32,256]{2,1,3,0:T(8,128)(2,1)S(1)} copy(bf16[1,32,32,256]{3,1,0,2:T(8,128)(2,1)} %get-tuple-element.23) | data formatting | bytes 1048576
  329.2 6.6 %fusion.11 = f32[256,32,16,4]{1,2,3,0:T(8,128)} fusion(bf16[16,2,4,32,256]{3,0,2,4,1:T(8,128)(2,1)} %bitcast.110, bf16[1,32,32,256]{2,1,3,0:T(8,128)(2,1)S(1)} %copy.97), kind=kOutput, calls=%fused_computation.22 | convolution fusion | flops 33554432 | bytes 6815744 | tf_op jit(solution)/shard_map/arf,lkrf->lakf/dot_general | solution.py:23
  335.8 6.7 %fusion.8 = f32[256,32,16,4]{1,2,3,0:T(8,128)} fusion(bf16[16,2,4,32,256]{3,0,2,4,1:T(8,128)(2,1)} %bitcast.111, bf16[1,32,32,256]{2,1,3,0:T(8,128)(2,1)S(1)} %copy.97), kind=kOutput, calls=%fused_computation.19 | convolution fusion | flops 33554432 | bytes 6815744 | tf_op jit(solution)/shard_map/arf,lkrf->lakf/dot_general | solution.py:23
  342.5 4.5 copy.98
  346.9 9.1 %subtract_bitcast_fusion = f32[16,32,4,256]{1,0,2,3:T(8,128)} fusion(f32[256,32,16,4]{1,2,3,0:T(8,128)} %fusion.11, bf16[16,2,4,32,256]{3,0,2,4,1:T(8,128)(2,1)} %bitcast.112, bf16[1,32,32,256]{2,1,3,0:T(8,128)(2,1)S(1)} %copy.98), kind=kOutput, calls=%fused_computation.6 | convolution fusion | flops 34078720 | bytes 15204352 | tf_op jit(solution)/shard_map/arf,lkrf->lakf/dot_general | solution.py:23
  356.1 7.4 %copy.81 = f32[16,32,4,256]{3,1,2,0:T(8,128)} copy(f32[16,32,4,256]{1,0,2,3:T(8,128)} %subtract_bitcast_fusion) | data formatting | bytes 4194304 | tf_op jit(solution)/shard_map/sub | solution.py:70
  363.4 9.1 %negate_bitcast_fusion = f32[16,32,4,256]{1,0,2,3:T(8,128)} fusion(f32[256,32,16,4]{1,2,3,0:T(8,128)} %fusion.8, bf16[16,2,4,32,256]{3,0,2,4,1:T(8,128)(2,1)} %bitcast.113, bf16[1,32,32,256]{2,1,3,0:T(8,128)(2,1)S(1)} %copy.98), kind=kOutput, calls=%fused_computation.7 | convolution fusion | flops 34603008 | bytes 15204352 | tf_op jit(solution)/shard_map/arf,lkrf->lakf/dot_general | solution.py:23
  372.6 7.6 %copy.80 = f32[16,32,4,256]{3,1,2,0:T(8,128)} copy(f32[16,32,4,256]{1,0,2,3:T(8,128)} %negate_bitcast_fusion) | data formatting | bytes 4194304 | tf_op jit(solution)/shard_map/neg | solution.py:69
  380.2 9.6 %fusion.2 = f32[16,32,4,512]{3,1,2,0:T(8,128)} fusion(f32[16,32,4,256]{3,1,2,0:T(8,128)S(1)} %copy-done.3, f32[16,32,4,256]{3,1,2,0:T(8,128)} %copy.80, f32[512,256]{1,0:T(8,128)S(1)} %get-tuple-element.28, f32[512,256]{1,0:T(8,128)S(1)} %get-tuple-element.29), kind=kOutput, calls=%fused_computation.10 | convolution fusion | flops 6443761664 | bytes 9437184 | tf_op jit(solution)/shard_map/dot_general | solution.py:74
  389.8 4.3 broadcast_in_dim.18
  394.1 8.1 %scatter_fusion = f32[32,32,4,512]{3,1,2,0:T(8,128)} fusion(f32[32,32,4,512]{3,1,2,0:T(8,128)} %broadcast_in_dim.18, s32[16]{0:T(128)S(1)} %fusion.52, f32[16,32,4,512]{3,1,2,0:T(8,128)} %fusion.2), kind=kCustom, calls=%fused_computation.2 | custom fusion | bytes 12582976 | tf_op jit(solution)/shard_map/scatter | solution.py:75
  402.2 7.8 %all-to-all-start.1 = ((f32[32,32,4,512]{3,1,2,0:T(8,128)}), f32[32,32,4,512]{3,1,2,0:T(8,128)}, u32[]{:S(2)}, u32[]{:S(2)}) async-start(f32[32,32,4,512]{3,1,2,0:T(8,128)} %scatter_fusion), calls=%async_computation.2 | async-start | bytes 16777216 | tf_op jit(solution)/shard_map/all_to_all | solution.py:76
  410.9 187.1 %all-to-all-done.1 = f32[32,32,4,512]{3,1,2,0:T(8,128)} async-done(((f32[32,32,4,512]{3,1,2,0:T(8,128)}), f32[32,32,4,512]{3,1,2,0:T(8,128)}, u32[]{:S(2)}, u32[]{:S(2)}) %all-to-all-start.1) | async-done | bytes 8388640 | tf_op jit(solution)/shard_map/all_to_all | solution.py:76
  598.0 13.8 %copy.82 = f32[32,32,4,512]{3,2,1,0:T(4,128)} copy(f32[32,32,4,512]{3,1,2,0:T(8,128)} %all-to-all-done.1) | data formatting | bytes 16777216 | tf_op jit(solution)/shard_map/all_to_all | solution.py:76
  611.8 9.8 %reshape.108 = f32[32,65536]{1,0:T(8,128)} reshape(f32[32,32,4,512]{3,2,1,0:T(4,128)} %copy.82) | data formatting | bytes 16777216 | tf_op jit(solution)/shard_map/reshape | solution.py:77
  621.6 10.0 %dot_general.48 = f32[32,4,512,32]{2,1,0,3:T(4,128)} reshape(f32[65536,32]{0,1:T(8,128)} %bitcast.118) | data formatting | bytes 16777216 | tf_op jit(solution)/shard_map/dot_general | solution.py:78
  631.6 10.8 %fusion.61 = (bf16[2,32,4,512]{3,0,2,1:T(2,128)(2,1)S(1)}, f32[2,32,4,512]{3,0,2,1:T(2,128)S(1)}) fusion(f32[32,4,512,32]{2,1,0,3:T(4,128)} %dot_general.48, pred[32]{0:T(512)(128)(4,1)S(1)} %get-tuple-element.18, s32[32]{0:T(128)S(1)} %fusion.44, f32[2,32,4,512]{3,2,1,0:T(4,128)S(1)} %copy-done.5), kind=kOutput, calls=%fused_computation.86 | convolution fusion | flops 50724992 | bytes 9699488 | tf_op jit(solution)/shard_map/dot_general | solution.py:78
  (42 shorter events, 16.5 us)
Async XLA Ops:
  21.3 9.2 %copy-start.4 = (bf16[1,16,2,4,32,256]{5,4,3,2,1,0:T(8,128)(2,1)S(1)}, bf16[1,16,2,4,32,256]{5,4,3,2,1,0:T(8,128)(2,1)}, u32[]{:S(2)}) copy-start(bf16[1,16,2,4,32,256]{5,4,3,2,1,0:T(8,128)(2,1)} %param.5) | copy-start | bytes 6291460
  21.3 104.9 %all-to-all-start = ((bf16[32,32,4,512]{3,2,1,0:T(4,128)(2,1)}), bf16[32,32,4,512]{3,2,1,0:T(4,128)(2,1)}, u32[]{:S(2)}, u32[]{:S(2)}) async-start(bf16[32,32,4,512]{3,2,1,0:T(4,128)(2,1)} %broadcast_select_fusion), calls=%async_computation | async-start | bytes 8388608 | tf_op jit(solution)/shard_map/all_to_all | solution.py:46
  30.2 228.6 %reduce-scatter.2.cloned.1.call-start = ((), (), s32[]{:S(2)}) async-start(), calls=%async_computation.3 | async-start | bytes 2359296 | tf_op jit(solution)/shard_map/reduce_scatter | solution.py:62
  30.5 12.0 %copy-start.7 = (s32[32,16]{0,1:T(8,128)S(1)}, s32[32,16]{0,1:T(8,128)}, u32[]{:S(2)}) copy-start(s32[32,16]{0,1:T(8,128)} %param.7) | copy-start | bytes 6148
  145.6 6.9 %copy-start = (bf16[16,32,4,256]{1,0,2,3:T(8,128)(2,1)S(1)}, bf16[16,32,4,256]{1,0,2,3:T(8,128)(2,1)}, u32[]{:S(2)}) copy-start(bf16[16,32,4,256]{1,0,2,3:T(8,128)(2,1)} %copy.73) | copy-start | bytes 3145732
  145.6 10.6 %slice-start = ((s8[8388608]{0:T(1024)(128)(4,1)}), s8[4194304]{0:T(1024)(128)(4,1)S(1)}, s32[]{:S(2)}) async-start(s8[8388608]{0:T(1024)(128)(4,1)} %bitcast.114), calls=%async_computation.5 | async-start | bytes 8388608
  152.5 3.7 slice-start.1
  156.2 5.7 copy-start.1
  161.9 3.2 copy-start.2
  171.6 87.2 %copy-start.6 = (bf16[1,2,32,4,256]{4,3,2,1,0:T(4,128)(2,1)S(1)}, bf16[1,2,32,4,256]{4,3,2,1,0:T(4,128)(2,1)}, u32[]{:S(2)}) copy-start(bf16[1,2,32,4,256]{4,3,2,1,0:T(4,128)(2,1)} %param.6) | copy-start | bytes 393220
  179.6 132.8 %all-gather.2.cloned.1.call-start = ((), (), s32[]{:S(2)}) async-start(), calls=%async_computation.4 | async-start | bytes 1179648 | tf_op jit(solution)/shard_map/all_gather | solution.py:64
  372.6 7.6 %copy-start.3 = (f32[16,32,4,256]{3,1,2,0:T(8,128)S(1)}, f32[16,32,4,256]{3,1,2,0:T(8,128)}, u32[]{:S(2)}) copy-start(f32[16,32,4,256]{3,1,2,0:T(8,128)} %copy.81) | copy-start | bytes 6291460
  402.2 195.8 %all-to-all-start.1 = ((f32[32,32,4,512]{3,1,2,0:T(8,128)}), f32[32,32,4,512]{3,1,2,0:T(8,128)}, u32[]{:S(2)}, u32[]{:S(2)}) async-start(f32[32,32,4,512]{3,1,2,0:T(8,128)} %scatter_fusion), calls=%async_computation.2 | async-start | bytes 16777216 | tf_op jit(solution)/shard_map/all_to_all | solution.py:76
  621.6 10.0 %copy-start.5 = (f32[2,32,4,512]{3,2,1,0:T(4,128)S(1)}, f32[2,32,4,512]{3,2,1,0:T(4,128)}, u32[]{:S(2)}) copy-start(f32[2,32,4,512]{3,2,1,0:T(4,128)} %param.4) | copy-start | bytes 1572868
Sparse Core Ops, SparseCore 0:
  179.7 79.0 reduce-scatter.1
  262.1 50.2 all-gather.1
where the time goes:
time: 656 us; the launch traced here: 651 us
  waiting for transfers between devices  400 us (61%)
  local copies, waits for them, and re-layouts  129 us (20%)
  matrix products  72.7 us (11%)
  other arithmetic  18.7 us (3%)
  starting transfers between devices  17 us (3%)
  between operations  14.7 us (2%)
    all_to_all x1, waiting for transfers between devices, per_device(): lax.all_to_all(returning, 'target', split_axis=0, concat_axis=0, tiled=True)  187 us
    all_to_all x1, waiting for transfers between devices, per_device(): lax.all_to_all(outgoing, 'target', split_axis=0, concat_axis=0, tiled=True)  81.4 us
    reduce_scatter x1, waiting for transfers between devices, per_device(): lax.psum_scatter(partial_value, 'surface', scatter_dimension=2, tiled=True)  79.2 us
    all_gather x1, waiting for transfers between devices, per_device(): lax.all_gather(residual_share.astype(jnp.bfloat16), 'surface', axis=2, ti...  51.9 us
    unnamed x26, local copies, waits for them, and re-layouts  33.6 us
    dot_general x4, matrix products, correlate(): jnp.einsum('arf,lkrf->lakf', misfit_part, listed, preferred_element_type=...  31.6 us
    dot_general x4, matrix products, contract(): jnp.einsum('lakf,lkrf->arf', spec, listed, preferred_element_type=jnp.flo...  19.5 us
    all_to_all x1, local copies, waits for them, and re-layouts, per_device(): lax.all_to_all(returning, 'target', split_axis=0, concat_axis=0, tiled=True)  13.8 us
  transfers between devices with their start and end apart: 4, of which 4 were waited for; matrix products, arithmetic and copies ran while one was open for 2% of the time, Pallas kernels for 0%

commit v1 on v0

--- a/solution.py
+++ b/solution.py
@@ -5,6 +5,13 @@
 from jax.sharding import PartitionSpec as P
 
 step_length = 0.5
+
+
+def gather_over(array, mesh_axis, dim):
+    devices = lax.axis_size(mesh_axis)
+    blocks = jnp.stack([array for _ in range(devices)])
+    blocks = lax.all_to_all(blocks, mesh_axis, split_axis=0, concat_axis=0)
+    return jnp.concatenate(blocks, axis=dim)
 
 
 def make_table(samples):
@@ -61,7 +68,7 @@
     observed_share = observed[0].astype(jnp.float32)
     summed_share = lax.psum_scatter(partial_value, "surface", scatter_dimension=2, tiled=True)
     residual_share = observed_share - summed_share
-    misfit = lax.all_gather(residual_share.astype(jnp.bfloat16), "surface", axis=2, tiled=True)
+    misfit = gather_over(residual_share.astype(jnp.bfloat16), "surface", 2)
     misfit_real = misfit[0]
     misfit_imag = misfit[1]
     grad_spectra = jnp.concatenate(

time: 656 us -> 622 us (0.948)
  waiting for transfers between devices: 400 us -> 348 us
  blocking collectives: 0 us -> 29.8 us
  local copies, waits for them, and re-layouts: 129 us -> 117 us
    all_gather x1 -> x0, waiting for transfers between devices: 51.9 us -> none  [per_device(): lax.all_gather(residual_share.astype(jnp.bfloat16), 'surface', axis=2, ti...]
    all_to_all x0 -> x1, blocking collectives: none -> 29.8 us  [gather_over(): blocks = lax.all_to_all(blocks, mesh_axis, split_axis=0, concat_axis=0)]
    unnamed x26 -> x24, local copies, waits for them, and re-layouts: 33.6 us -> 14.6 us
    squeeze x0 -> x2, local copies, waits for them, and re-layouts: none -> 8.91 us  [the longest x1 4.45 us: per_device(): misfit_real = misfit[0]]
  transfers between devices with their start and end apart: 4 -> 3, of which waited for: 4 -> 3; matrix products, arithmetic and copies ran while one was open for 2% -> 2% of each run, Pallas kernels for 0% -> 0%
where the time goes in v1:
time: 622 us; the launch traced here: 618 us
  waiting for transfers between devices  348 us (56%)
  local copies, waits for them, and re-layouts  117 us (19%)
  matrix products  72.7 us (12%)
  blocking collectives  29.8 us (5%)
  other arithmetic  18 us (3%)
  starting transfers between devices  17.2 us (3%)
  between operations  14.7 us (2%)
    all_to_all x1, waiting for transfers between devices, per_device(): lax.all_to_all(returning, 'target', split_axis=0, concat_axis=0, tiled=True)  187 us
    all_to_all x1, waiting for transfers between devices, per_device(): lax.all_to_all(outgoing, 'target', split_axis=0, concat_axis=0, tiled=True)  81.4 us
    reduce_scatter x1, waiting for transfers between devices, per_device(): lax.psum_scatter(partial_value, 'surface', scatter_dimension=2, tiled=True)  79.2 us
    dot_general x4, matrix products, correlate(): jnp.einsum('arf,lkrf->lakf', misfit_part, listed, preferred_element_type=...  31.5 us
    all_to_all x1, blocking collectives, gather_over(): blocks = lax.all_to_all(blocks, mesh_axis, split_axis=0, concat_axis=0)  29.8 us
    dot_general x4, matrix products, contract(): jnp.einsum('lakf,lkrf->arf', spec, listed, preferred_element_type=jnp.flo...  19.5 us
    unnamed x24, local copies, waits for them, and re-layouts  14.6 us
    all_to_all x1, local copies, waits for them, and re-layouts, per_device(): lax.all_to_all(returning, 'target', split_axis=0, concat_axis=0, tiled=True)  13.8 us
  transfers between devices with their start and end apart: 3, of which 3 were waited for; matrix products, arithmetic and copies ran while one was open for 2% of the time, Pallas kernels for 0%

profile of v1, /device:TPU:96, one launch (start us, length us, event | category | flops | bytes accessed | tf_op | source)
XLA Modules:
  0.0 617.5 jit_solution(1214215365610578129)
XLA Ops:
  9.8 5.6 gather_fusion
  15.4 5.9 broadcast_select_fusion
  21.3 8.9 %all-to-all-start = ((bf16[32,32,4,512]{3,2,1,0:T(4,128)(2,1)}), bf16[32,32,4,512]{3,2,1,0:T(4,128)(2,1)}, u32[]{:S(2)}, u32[]{:S(2)}) async-start(bf16[32,32,4,512]{3,2,1,0:T(4,128)(2,1)} %broadcast_select_fusion), calls=%async_computation | async-start | bytes 8388608 | tf_op jit(solution)/shard_map/all_to_all | solution.py:53
  30.5 12.0 %copy.82 = bf16[1,16,2,4,32,256]{4,1,3,5,2,0:T(8,128)(2,1)} copy(bf16[1,16,2,4,32,256]{5,4,3,2,1,0:T(8,128)(2,1)S(1)} %copy-done.4) | data formatting | bytes 4194304 | tf_op args[1]
  44.8 81.4 %all-to-all-done = bf16[32,32,4,512]{3,2,1,0:T(4,128)(2,1)} async-done(((bf16[32,32,4,512]{3,2,1,0:T(4,128)(2,1)}), bf16[32,32,4,512]{3,2,1,0:T(4,128)(2,1)}, u32[]{:S(2)}, u32[]{:S(2)}) %all-to-all-start) | async-done | bytes 4194336 | tf_op jit(solution)/shard_map/all_to_all | solution.py:53
  126.2 4.5 gather_fusion.1
  132.3 6.5 %copy.83 = bf16[16,32,4,256]{1,0,2,3:T(8,128)(2,1)} copy(bf16[16,32,4,256]{3,1,2,0:T(8,128)(2,1)S(1)} %get-tuple-element.20) | data formatting | bytes 2097152 | tf_op jit(solution)/shard_map/slice | solution.py:58
  138.8 6.7 %copy.84 = bf16[16,32,4,256]{1,0,2,3:T(8,128)(2,1)} copy(bf16[16,32,4,256]{3,1,2,0:T(8,128)(2,1)S(1)} %get-tuple-element.21) | data formatting | bytes 2097152 | tf_op jit(solution)/shard_map/slice | solution.py:59
  145.6 6.9 %fusion.9 = f32[256,32,32,1]{2,1,3,0:T(8,128)} fusion(bf16[16,32,4,256]{1,0,2,3:T(8,128)(2,1)} %copy.84, bf16[16,2,4,32,256]{3,0,2,4,1:T(8,128)(2,1)} %bitcast.107), kind=kOutput, calls=%fused_computation.20 | convolution fusion | flops 33554432 | bytes 9437184 | tf_op jit(solution)/shard_map/lakf,lkrf->arf/dot_general | solution.py:26
  152.4 3.7 fusion.10
  156.2 5.7 fusion.6
  165.1 6.5 %pad_maximum_fusion = f32[2,32,32,256]{2,1,3,0:T(8,128)} fusion(f32[1,32,32,256]{2,1,3,0:T(8,128)S(1)} %copy-done.2, f32[1,32,32,256]{2,1,3,0:T(8,128)} %fusion.7), kind=kLoop, calls=%fused_computation.3 | loop fusion | flops 524288 | bytes 4194304 | tf_op jit(solution)/shard_map/stack | solution.py:62
  171.6 7.9 %copy.87 = f32[2,32,32,256]{3,1,0,2:T(8,128)} copy(f32[2,32,32,256]{2,1,3,0:T(8,128)} %pad_maximum_fusion) | data formatting | bytes 4194304 | tf_op jit(solution)/shard_map/stack | solution.py:62
  179.6 79.2 %reduce-scatter.2.cloned.1.call-done = f32[2,32,4,256]{3,1,0,2:T(8,128)} async-done(((f32[2,32,32,256]{3,1,0,2:T(8,128)}), f32[2,32,4,256]{3,1,0,2:T(8,128)}) %reduce-scatter.2.cloned.1.call-update) | async-done | bytes 262160 | tf_op jit(solution)/shard_map/reduce_scatter | solution.py:69
  259.9 29.8 %all_to_all.15 = bf16[8,2,32,4,256]{4,2,3,1,0:T(8,128)(2,1)S(1)} all-to-all(bf16[8,2,32,4,256]{4,2,3,1,0:T(8,128)(2,1)S(1)} %stack.11), channel_id=1, replica_groups=mesh['target'=32,'surface'=8] {'surface'}, dimensions={0} | all-to-all | bytes 2097152 | tf_op jit(solution)/shard_map/all_to_all | solution.py:13
  290.9 4.5 copy.107
  295.4 6.6 %fusion.11 = f32[256,32,16,4]{1,2,3,0:T(8,128)} fusion(bf16[32,32,256,1]{1,0,3,2:T(8,128)(2,1)S(1)} %copy.107, bf16[16,2,4,32,256]{3,0,2,4,1:T(8,128)(2,1)} %bitcast.109), kind=kOutput, calls=%fused_computation.22 | convolution fusion | flops 33554432 | bytes 6815744 | tf_op jit(solution)/shard_map/arf,lkrf->lakf/dot_general | solution.py:30
  302.0 6.7 %fusion.8 = f32[256,32,16,4]{1,2,3,0:T(8,128)} fusion(bf16[32,32,256,1]{1,0,3,2:T(8,128)(2,1)S(1)} %copy.107, bf16[16,2,4,32,256]{3,0,2,4,1:T(8,128)(2,1)} %bitcast.110), kind=kOutput, calls=%fused_computation.19 | convolution fusion | flops 33554432 | bytes 6815744 | tf_op jit(solution)/shard_map/arf,lkrf->lakf/dot_general | solution.py:30
  308.7 4.5 copy.108
  313.1 9.1 %subtract_bitcast_fusion = f32[16,32,4,256]{1,0,2,3:T(8,128)} fusion(f32[256,32,16,4]{1,2,3,0:T(8,128)} %fusion.11, bf16[32,32,256,1]{1,0,3,2:T(8,128)(2,1)S(1)} %copy.108, bf16[16,2,4,32,256]{3,0,2,4,1:T(8,128)(2,1)} %bitcast.111), kind=kOutput, calls=%fused_computation.6 | convolution fusion | flops 34078720 | bytes 15204352 | tf_op jit(solution)/shard_map/arf,lkrf->lakf/dot_general | solution.py:30
  322.2 7.4 %copy.95 = f32[16,32,4,256]{3,1,2,0:T(8,128)} copy(f32[16,32,4,256]{1,0,2,3:T(8,128)} %subtract_bitcast_fusion) | data formatting | bytes 4194304 | tf_op jit(solution)/shard_map/sub | solution.py:77
  329.6 9.1 %negate_bitcast_fusion = f32[16,32,4,256]{1,0,2,3:T(8,128)} fusion(f32[256,32,16,4]{1,2,3,0:T(8,128)} %fusion.8, bf16[32,32,256,1]{1,0,3,2:T(8,128)(2,1)S(1)} %copy.108, bf16[16,2,4,32,256]{3,0,2,4,1:T(8,128)(2,1)} %bitcast.112), kind=kOutput, calls=%fused_computation.7 | convolution fusion | flops 34603008 | bytes 15204352 | tf_op jit(solution)/shard_map/arf,lkrf->lakf/dot_general | solution.py:30
  338.7 7.5 %copy.94 = f32[16,32,4,256]{3,1,2,0:T(8,128)} copy(f32[16,32,4,256]{1,0,2,3:T(8,128)} %negate_bitcast_fusion) | data formatting | bytes 4194304 | tf_op jit(solution)/shard_map/neg | solution.py:76
  346.3 9.6 %fusion.2 = f32[16,32,4,512]{3,1,2,0:T(8,128)} fusion(f32[16,32,4,256]{3,1,2,0:T(8,128)S(1)} %copy-done.3, f32[16,32,4,256]{3,1,2,0:T(8,128)} %copy.94, f32[512,256]{1,0:T(8,128)S(1)} %get-tuple-element.28, f32[512,256]{1,0:T(8,128)S(1)} %get-tuple-element.29), kind=kOutput, calls=%fused_computation.10 | convolution fusion | flops 6443761664 | bytes 9437184 | tf_op jit(solution)/shard_map/dot_general | solution.py:81
  355.8 4.3 broadcast_in_dim.18
  360.2 8.0 %scatter_fusion = f32[32,32,4,512]{3,1,2,0:T(8,128)} fusion(f32[32,32,4,512]{3,1,2,0:T(8,128)} %broadcast_in_dim.18, s32[16]{0:T(128)S(1)} %fusion.48, f32[16,32,4,512]{3,1,2,0:T(8,128)} %fusion.2), kind=kCustom, calls=%fused_computation.2 | custom fusion | bytes 12582976 | tf_op jit(solution)/shard_map/scatter | solution.py:82
  368.1 8.0 %all-to-all-start.2 = ((f32[32,32,4,512]{3,1,2,0:T(8,128)}), f32[32,32,4,512]{3,1,2,0:T(8,128)}, u32[]{:S(2)}, u32[]{:S(2)}) async-start(f32[32,32,4,512]{3,1,2,0:T(8,128)} %scatter_fusion), calls=%async_computation.3 | async-start | bytes 16777216 | tf_op jit(solution)/shard_map/all_to_all | solution.py:83
  377.0 187.1 %all-to-all-done.2 = f32[32,32,4,512]{3,1,2,0:T(8,128)} async-done(((f32[32,32,4,512]{3,1,2,0:T(8,128)}), f32[32,32,4,512]{3,1,2,0:T(8,128)}, u32[]{:S(2)}, u32[]{:S(2)}) %all-to-all-start.2) | async-done | bytes 8388640 | tf_op jit(solution)/shard_map/all_to_all | solution.py:83
  564.1 13.8 %copy.96 = f32[32,32,4,512]{3,2,1,0:T(4,128)} copy(f32[32,32,4,512]{3,1,2,0:T(8,128)} %all-to-all-done.2) | data formatting | bytes 16777216 | tf_op jit(solution)/shard_map/all_to_all | solution.py:83
  577.9 9.8 %reshape.119 = f32[32,65536]{1,0:T(8,128)} reshape(f32[32,32,4,512]{3,2,1,0:T(4,128)} %copy.96) | data formatting | bytes 16777216 | tf_op jit(solution)/shard_map/reshape | solution.py:84
  587.7 10.0 %dot_general.48 = f32[32,4,512,32]{2,1,0,3:T(4,128)} reshape(f32[65536,32]{0,1:T(8,128)} %bitcast.117) | data formatting | bytes 16777216 | tf_op jit(solution)/shard_map/dot_general | solution.py:85
  597.7 10.8 %fusion.57 = (bf16[2,32,4,512]{3,0,2,1:T(2,128)(2,1)S(1)}, f32[2,32,4,512]{3,0,2,1:T(2,128)S(1)}) fusion(f32[32,4,512,32]{2,1,0,3:T(4,128)} %dot_general.48, pred[32]{0:T(512)(128)(4,1)S(1)} %get-tuple-element.18, s32[32]{0:T(128)S(1)} %fusion.40, f32[2,32,4,512]{3,2,1,0:T(4,128)S(1)} %copy-done.5), kind=kOutput, calls=%fused_computation.83 | convolution fusion | flops 50724992 | bytes 9699488 | tf_op jit(solution)/shard_map/dot_general | solution.py:85
  (43 shorter events, 14.9 us)
Async XLA Ops:
  21.3 9.2 %copy-start.4 = (bf16[1,16,2,4,32,256]{5,4,3,2,1,0:T(8,128)(2,1)S(1)}, bf16[1,16,2,4,32,256]{5,4,3,2,1,0:T(8,128)(2,1)}, u32[]{:S(2)}) copy-start(bf16[1,16,2,4,32,256]{5,4,3,2,1,0:T(8,128)(2,1)} %param.5) | copy-start | bytes 6291460
  21.3 104.9 %all-to-all-start = ((bf16[32,32,4,512]{3,2,1,0:T(4,128)(2,1)}), bf16[32,32,4,512]{3,2,1,0:T(4,128)(2,1)}, u32[]{:S(2)}, u32[]{:S(2)}) async-start(bf16[32,32,4,512]{3,2,1,0:T(4,128)(2,1)} %broadcast_select_fusion), calls=%async_computation | async-start | bytes 8388608 | tf_op jit(solution)/shard_map/all_to_all | solution.py:53
  30.2 228.5 %reduce-scatter.2.cloned.1.call-start = ((), (), s32[]{:S(2)}) async-start(), calls=%async_computation.4 | async-start | bytes 2359296 | tf_op jit(solution)/shard_map/reduce_scatter | solution.py:69
  30.5 12.0 %copy-start.7 = (s32[32,16]{0,1:T(8,128)S(1)}, s32[32,16]{0,1:T(8,128)}, u32[]{:S(2)}) copy-start(s32[32,16]{0,1:T(8,128)} %param.7) | copy-start | bytes 6148
  145.6 6.9 %copy-start = (bf16[16,32,4,256]{1,0,2,3:T(8,128)(2,1)S(1)}, bf16[16,32,4,256]{1,0,2,3:T(8,128)(2,1)}, u32[]{:S(2)}) copy-start(bf16[16,32,4,256]{1,0,2,3:T(8,128)(2,1)} %copy.83) | copy-start | bytes 3145732
  145.6 10.6 %slice-start = ((s8[8388608]{0:T(1024)(128)(4,1)}), s8[4194304]{0:T(1024)(128)(4,1)S(1)}, s32[]{:S(2)}) async-start(s8[8388608]{0:T(1024)(128)(4,1)} %bitcast.113), calls=%async_computation.5 | async-start | bytes 8388608
  152.4 3.7 slice-start.1
  156.2 5.7 copy-start.1
  161.9 3.3 copy-start.2
  171.6 87.2 %copy-start.6 = (bf16[1,2,32,4,256]{4,3,2,1,0:T(4,128)(2,1)S(1)}, bf16[1,2,32,4,256]{4,3,2,1,0:T(4,128)(2,1)}, u32[]{:S(2)}) copy-start(bf16[1,2,32,4,256]{4,3,2,1,0:T(4,128)(2,1)} %param.6) | copy-start | bytes 393220
  338.7 7.6 %copy-start.3 = (f32[16,32,4,256]{3,1,2,0:T(8,128)S(1)}, f32[16,32,4,256]{3,1,2,0:T(8,128)}, u32[]{:S(2)}) copy-start(f32[16,32,4,256]{3,1,2,0:T(8,128)} %copy.95) | copy-start | bytes 6291460
  368.1 196.0 %all-to-all-start.2 = ((f32[32,32,4,512]{3,1,2,0:T(8,128)}), f32[32,32,4,512]{3,1,2,0:T(8,128)}, u32[]{:S(2)}, u32[]{:S(2)}) async-start(f32[32,32,4,512]{3,1,2,0:T(8,128)} %scatter_fusion), calls=%async_computation.3 | async-start | bytes 16777216 | tf_op jit(solution)/shard_map/all_to_all | solution.py:83
  587.7 10.0 %copy-start.5 = (f32[2,32,4,512]{3,2,1,0:T(4,128)S(1)}, f32[2,32,4,512]{3,2,1,0:T(4,128)}, u32[]{:S(2)}) copy-start(f32[2,32,4,512]{3,2,1,0:T(4,128)} %param.4) | copy-start | bytes 1572868
Sparse Core Ops, SparseCore 0:
  179.7 79.0 reduce-scatter.1
